TPU v7x, 256 devices: a whole 4x4x8 slice. The times are simulated.
256 devices in a mesh: pair: 16 (over z, core), virt: 16 (over x, y).
Axes of the slice: x: 4, y: 4, z: 8, core: 2. Of those that a mesh axis runs over, the one named last changes fastest.
Arguments:
- amplitudes: float32 [64, 2048, 4096], P('virt', 'pair'), may hold values from -0.9 to 0.9
- integrals: float32 [64, 384, 4096], P('virt', 'pair'), may hold values from -0.09375 to 0.09375
- tile_flags: int32 [64], P('virt'), may hold values 0 or 1
- live_count: int32 [16], replicated, may hold values from 1 to 4, as said below
- pair_occ: int32 [2048, 2], P(('pair', 'virt')), may hold values from 0 to 199
- occ_energy: float32 [200], replicated, may hold values from -2.5 to -0.3
- ab_energy: float32 [384], replicated, may hold values from 0.6 to 3
Outputs:
- ladder: float32 [2048, 384], P(('pair', 'virt'))
- update: float32 [2048, 384], P(('pair', 'virt'))
Inputs may be any that keep to these rules, and one draw needn't show every extreme that they name: `live_count`: entry v is how many of the 4 slots of virt index v hold tile pairs: its slots below that number do, and the contents of the others are not to be used. At some index it is 4, and at the index half the axis away it is 1.
All inputs are finite; a program needn't handle non-finite values. No bound on the sum of `tile_flags` on one device may be relied on, other than what follows from the above.
Results may differ from a plain program's by a relative error of at most 0.0001.
Values sent between devices are 32-bit elements; how exact they have to be, the bound alone decides.
No kernel may reach another device: no remote copies, remote signals or barrier semaphores. Data moves between devices by JAX's collectives and lax.ppermute only.
A program may use at most 128 MiB of HBM per device.

v0:
```python
import jax
import jax.numpy as jnp
from jax import lax
from jax.sharding import PartitionSpec as P

TILE = 64


def swap_in_tile(rows):
    shaped = rows.reshape(rows.shape[0], TILE, TILE)
    return jnp.swapaxes(shaped, 1, 2).reshape(rows.shape)


def symmetric_amps(amp_rows, flag):
    return amp_rows + flag.astype(jnp.float32) * swap_in_tile(amp_rows)


def tile_product(amp_tile, int_rows, precision=lax.Precision.HIGH):
    return lax.dot_general(
        amp_tile,
        int_rows,
        (((1,), (1,)), ((), ())),
        precision=precision,
        preferred_element_type=jnp.float32,
    )


def on_device(amplitudes, integrals, tile_flags, live_count, pair_occ, occ_energy, ab_energy):
    slots, pair_rows, _ = amplitudes.shape
    n_virt = lax.axis_size("virt")
    half = n_virt // 2
    virt_index = lax.axis_index("virt")
    partner = (virt_index + half) % n_virt
    columns = jnp.arange(n_virt, dtype=jnp.int32)
    neighbour = columns ^ 1
    across = jnp.roll(live_count, half)
    give_one = jnp.clip((live_count - across) // 2, 0, 1)
    take_one = jnp.clip((across - live_count) // 2, 0, 1)
    keep_one = live_count - give_one
    give_two = ((keep_one == 4) & (take_one[neighbour] == 0) & (keep_one[neighbour] <= 2)).astype(
        jnp.int32
    )
    take_two = give_two[neighbour]
    keep_all = keep_one - give_two
    own_count = live_count[virt_index]
    take = take_one[virt_index]
    take_y = take_two[virt_index]
    keep = keep_all[virt_index]
    send_at = own_count - 1
    send_amp = symmetric_amps(
        lax.dynamic_index_in_dim(amplitudes, send_at, 0, keepdims=False),
        lax.dynamic_index_in_dim(tile_flags, send_at, 0, keepdims=False),
    )
    send_int = lax.dynamic_index_in_dim(integrals, send_at, 0, keepdims=False)
    perm = [(v, (v + half) % n_virt) for v in range(n_virt)]
    recv_int = lax.ppermute(send_int, "virt", perm)
    recv_amp = lax.ppermute(send_amp, "virt", perm)
    perm_y = [(v, v ^ 1) for v in range(n_virt)]
    recv_int_y = lax.ppermute(integrals[3], "virt", perm_y)
    recv_amp_y = lax.ppermute(symmetric_amps(amplitudes[3], tile_flags[3]), "virt", perm_y)

    def own_amps(slot):
        return symmetric_amps(amplitudes[slot], tile_flags[slot])

    first_two = lax.all_gather(integrals[0:2], "pair", axis=1, tiled=True)
    running = tile_product(own_amps(0), first_two[0], lax.Precision.HIGHEST)
    second = tile_product(own_amps(1), first_two[1], lax.Precision.HIGHEST)
    running = running + jnp.where(keep > 1, second, jnp.zeros_like(second))
    third_int = jnp.where(take > 0, recv_int, jnp.where(take_y > 0, recv_int_y, integrals[2]))
    third_amp = jnp.where(take > 0, recv_amp, jnp.where(take_y > 0, recv_amp_y, own_amps(2)))
    third = tile_product(third_amp, lax.all_gather(third_int, "pair", axis=0, tiled=True))
    third_live = (take > 0) | (take_y > 0) | (keep > 2)
    running = running + jnp.where(third_live, third, jnp.zeros_like(third))

    def fourth(acc):
        gathered = lax.all_gather(integrals[3], "pair", axis=0, tiled=True)
        term = tile_product(own_amps(3), gathered)
        return acc + jnp.where(keep > 3, term, jnp.zeros_like(term))

    any_full = jnp.max(keep_all) > 3
    running = lax.cond(any_full, fourth, lambda acc: acc, running)
    ab = running.shape[1]
    blocks = running.reshape(n_virt, pair_rows // n_virt, ab)
    received = lax.all_to_all(blocks, "virt", 0, 0, tiled=False)
    ladder = jnp.sum(received, axis=0)
    occ_range = jnp.arange(occ_energy.shape[0], dtype=jnp.int32)
    first_energy = jnp.sum(
        jnp.where(pair_occ[:, 0:1] == occ_range[None, :], occ_energy[None, :], 0.0), axis=1
    )
    second_energy = jnp.sum(
        jnp.where(pair_occ[:, 1:2] == occ_range[None, :], occ_energy[None, :], 0.0), axis=1
    )
    denominator = ab_energy[None, :] - first_energy[:, None] - second_energy[:, None]
    return (ladder, ladder / denominator)


def solution(mesh):
    return jax.shard_map(
        on_device,
        mesh=mesh,
        in_specs=(
            P("virt", "pair", None),
            P("virt", "pair", None),
            P("virt"),
            P(),
            P(("pair", "virt"), None),
            P(),
            P(),
        ),
        out_specs=(P(("pair", "virt"), None), P(("pair", "virt"), None)),
        check_vma=False,
    )
```

profile of v0, /device:TPU:1, one launch (start us, length us, event | category | flops | bytes accessed | tf_op | source)
XLA Modules:
  0.0 164.5 jit_solution(631864503196057487)
XLA Ops:
  7.2 2.2 %slice.66 = f32[2,24,4096]{2,1,0:T(8,128)} slice(f32[4,24,4096]{2,1,0:T(8,128)} %param.10), slice={[0:2], [0:24], [0:4096]} | slice | bytes 1572864 | tf_op jit(solution)/shard_map/slice | solution.py:65
  9.5 0.6 dynamic_slice.27
  11.5 3.6 %collective-permute-start.2 = (f32[24,4096]{1,0:T(8,128)S(1)}, f32[24,4096]{1,0:T(8,128)S(1)}, u32[]{:S(2)}, u32[]{:S(2)}) collective-permute-start(f32[24,4096]{1,0:T(8,128)S(1)} %get-tuple-element.42), channel_id=1, source_target_pairs={{0,8},{1,9},{2,10},{3,11},{4,12},{5,13},{6,14},{7,15},{8,0},{9,1},... | collective-permute-start | bytes 1179656 | tf_op jit(solution)/shard_map/ppermute | solution.py:56
  15.1 1.3 collective-permute-start.3
  16.6 0.7 dynamic_slice.25
  17.2 0.7 gather_fusion
  17.9 0.7 gather_fusion.1
  18.6 0.6 fusion.24
  19.2 0.7 gather_fusion.2
  19.9 0.6 dynamic_slice.26
  21.8 1.1 collective-permute-done.2
  22.9 1.9 %collective-permute-done.3 = f32[24,4096]{1,0:T(8,128)S(1)} collective-permute-done((f32[24,4096]{1,0:T(8,128)S(1)}, f32[24,4096]{1,0:T(8,128)S(1)}, u32[]{:S(2)}, u32[]{:S(2)}) %collective-permute-start.3) | collective-permute-done | bytes 393248 | tf_op jit(solution)/shard_map/ppermute | solution.py:59
  24.8 0.8 fusion.21
  25.7 8.3 %fusion.25 = (f32[1,128,4096]{2,1,0:T(8,128)}, f32[1,128,4096]{2,1,0:T(8,128)}, f32[1,128,4096]{2,1,0:T(8,128)}, f32[1,128,4096]{2,1,0:T(8,128)}, f32[1,128,4096]{2,1,0:T(8,128)}) fusion(f32[4,128,4096]{2,1,0:T(8,128)} %param.9, s32[]{:T(128)S(6)} %select_n.101), kind=kLoop, calls=%fused_computation.59 | loop fusion | bytes 20971524 | tf_op jit(solution)/shard_map/slice | solution.py:63
  34.0 1.9 %copy.41 = f32[1,128,4096]{1,2,0:T(8,128)S(1)} copy(f32[1,128,4096]{2,1,0:T(8,128)} %get-tuple-element.38) | data formatting | bytes 4194304
  35.9 0.7 fusion.26
  37.2 0.1 broadcast_multiply_fusion.2
  37.4 1.2 copy.33
  38.6 1.7 %bitcast_add_fusion.3 = f32[128,4096]{0,1:T(8,128)} fusion(f32[128,64,64]{0,2,1:T(8,128)S(1)} %copy.33, f32[1,128,4096]{1,2,0:T(8,128)S(1)} %copy.41), kind=kLoop, calls=%fused_computation.17 | loop fusion | flops 524288 | bytes 6291456 | tf_op jit(solution)/shard_map/add | solution.py:15
  40.3 2.1 %collective-permute-start = (f32[128,4096]{0,1:T(8,128)}, f32[128,4096]{0,1:T(8,128)}, u32[]{:S(2)}, u32[]{:S(2)}) collective-permute-start(f32[128,4096]{0,1:T(8,128)} %bitcast_add_fusion.3), channel_id=1, source_target_pairs={{0,8},{1,9},{2,10},{3,11},{4,12},{5,13},{6,14},{7,15},{8,0},{9,1},... | collective-permute-start | bytes 6291464 | tf_op jit(solution)/shard_map/ppermute | solution.py:57
  42.4 1.9 %copy.42 = f32[1,128,4096]{1,2,0:T(8,128)S(1)} copy(f32[1,128,4096]{2,1,0:T(8,128)} %get-tuple-element.37) | data formatting | bytes 4194304
  44.9 0.1 broadcast_multiply_fusion.1
  45.1 1.2 copy.35
  46.3 1.6 bitcast_add_fusion.2
  47.8 1.2 collective-permute-start.1
  49.1 1.9 %copy.43 = f32[1,128,4096]{1,2,0:T(8,128)S(1)} copy(f32[1,128,4096]{2,1,0:T(8,128)} %get-tuple-element.36) | data formatting | bytes 4194304
  51.6 0.1 broadcast_multiply_fusion
  51.8 0.5 copy-done.1
  52.3 2.5 %copy.37 = f32[128,64,64]{0,2,1:T(8,128)} copy(f32[128,64,64]{0,1,2:T(8,128)S(1)} %bitcast.100) | data formatting | bytes 4194304 | tf_op jit(solution)/shard_map/mul | solution.py:15
  54.8 1.9 %copy.40 = f32[1,128,4096]{1,2,0:T(8,128)S(1)} copy(f32[1,128,4096]{2,1,0:T(8,128)} %get-tuple-element.39) | data formatting | bytes 4194304
  57.6 2.6 %copy.31 = f32[128,64,64]{0,2,1:T(8,128)} copy(f32[128,64,64]{0,1,2:T(8,128)S(1)} %bitcast.101) | data formatting | bytes 4194304 | tf_op jit(solution)/shard_map/mul | solution.py:15
  60.1 0.6 dynamic_slice.24
  60.7 2.9 %copy.39 = f32[1,128,4096]{1,2,0:T(8,128)} copy(f32[1,128,4096]{2,1,0:T(8,128)} %get-tuple-element.40) | data formatting | bytes 4194304
  64.2 1.8 %broadcast_multiply_fusion.4 = f32[1,128,4096]{1,2,0:T(8,128)S(1)} fusion(f32[1,128,4096]{1,2,0:T(8,128)} %copy.39, f32[]{:T(128)} %bitcast.7), kind=kLoop, calls=%fused_computation.30 | loop fusion | flops 524288 | bytes 4194308 | tf_op jit(solution)/shard_map/mul | solution.py:15
  66.0 2.5 %copy.29 = f32[128,64,64]{0,2,1:T(8,128)} copy(f32[128,64,64]{0,1,2:T(8,128)S(1)} %bitcast.102) | data formatting | bytes 4194304 | tf_op jit(solution)/shard_map/mul | solution.py:15
  70.5 3.4 %bitcast_add_fusion.4 = f32[1,128,4096]{1,2,0:T(8,128)} fusion(f32[1,128,4096]{1,2,0:T(8,128)S(1)} %copy.40, f32[128,64,64]{0,2,1:T(8,128)} %copy.31), kind=kLoop, calls=%fused_computation.19 | loop fusion | flops 524288 | bytes 6291456 | tf_op jit(solution)/shard_map/add | solution.py:15
  74.0 1.6 bitcast_add_fusion.5
  75.5 11.9 %collective-permute-done = f32[128,4096]{0,1:T(8,128)} collective-permute-done((f32[128,4096]{0,1:T(8,128)}, f32[128,4096]{0,1:T(8,128)}, u32[]{:S(2)}, u32[]{:S(2)}) %collective-permute-start) | collective-permute-done | bytes 2097184 | tf_op jit(solution)/shard_map/ppermute | solution.py:57
  87.4 6.4 %collective-permute-done.1 = f32[128,4096]{0,1:T(8,128)} collective-permute-done((f32[128,4096]{0,1:T(8,128)}, f32[128,4096]{0,1:T(8,128)}, u32[]{:S(2)}, u32[]{:S(2)}) %collective-permute-start.1) | collective-permute-done | bytes 2097184 | tf_op jit(solution)/shard_map/ppermute | solution.py:60
  93.8 2.3 %fusion.11 = f32[128,4096]{0,1:T(8,128)} fusion(f32[128,4096]{0,1:T(8,128)} %collective-permute-done, f32[128,4096]{0,1:T(8,128)} %collective-permute-done.1, f32[128,64,64]{0,2,1:T(8,128)S(1)} %copy-done.7, f32[1,128,4096]{1,2,0:T(8,128)S(1)} %copy-done.2, pred[]{:T(512)} %bitcast.21, pred[]{:T(512)} %bitcast.20), kind=kLoop, calls=%fused_computation.15 | loop fusion | flops 1572864 | bytes 10485762 | tf_op jit(solution)/shard_map/jit(_where)/select_n | solution.py:70
  96.1 9.5 %fusion.17 = f32[128,384]{1,0:T(8,128)S(1)} fusion(f32[2,384,4096]{2,1,0:T(8,128)} %all-gather.7.cloned.1.call-done, f32[1,128,4096]{1,2,0:T(8,128)S(1)} %copy-done.4, pred[]{:T(512)S(6)} %gt.29), kind=kOutput, calls=%fused_computation.23 | convolution fusion | flops 2415968256 | bytes 8585217 | tf_op jit(solution)/shard_map/dot_general | solution.py:19
  105.7 9.8 %fusion.14 = f32[128,384]{1,0:T(8,128)S(1)} fusion(f32[128,384]{1,0:T(8,128)S(1)} %fusion.17, f32[2,384,4096]{2,1,0:T(8,128)} %all-gather.7.cloned.1.call-done, f32[1,128,4096]{1,2,0:T(8,128)S(1)} %copy-done.5), kind=kOutput, calls=%fused_computation.22 | convolution fusion | flops 2415968256 | bytes 8781824 | tf_op jit(solution)/shard_map/dot_general | solution.py:19
  115.5 20.6 %all-gather.9.cloned.1.call-done = f32[384,4096]{1,0:T(8,128)} async-done(((f32[24,4096]{1,0:T(8,128)}), f32[384,4096]{1,0:T(8,128)}) %all-gather.9.cloned.1.call-update) | async-done | bytes 6291472 | tf_op jit(solution)/shard_map/all_gather | solution.py:71
  136.1 7.1 %fusion.20 = f32[128,384]{1,0:T(8,128)} fusion(f32[128,384]{1,0:T(8,128)S(1)} %fusion.14, f32[128,4096]{0,1:T(8,128)S(1)} %copy-done.6, f32[384,4096]{1,0:T(8,128)} %all-gather.9.cloned.1.call-done, pred[]{:T(512)S(6)} %or.7), kind=kOutput, calls=%fused_computation.25 | convolution fusion | flops 1208057856 | bytes 8781825 | tf_op jit(solution)/shard_map/dot_general | solution.py:19
  143.2 6.7 %all-to-all-start = ((f32[16,8,384]{2,1,0:T(8,128)}), f32[16,8,384]{2,1,0:T(8,128)S(1)}, u32[]{:S(2)}, u32[]{:S(2)}) async-start(f32[16,8,384]{2,1,0:T(8,128)} %bitcast.42), calls=%async_computation | async-start | bytes 393216 | tf_op jit(solution)/shard_map/all_to_all | solution.py:84
  149.9 0.2 select_reduce_fusion.1
  150.1 6.8 %all-to-all-done = f32[16,8,384]{2,1,0:T(8,128)S(1)} async-done(((f32[16,8,384]{2,1,0:T(8,128)}), f32[16,8,384]{2,1,0:T(8,128)S(1)}, u32[]{:S(2)}, u32[]{:S(2)}) %all-to-all-start) | async-done | bytes 196640 | tf_op jit(solution)/shard_map/all_to_all | solution.py:84
  156.9 0.7 subtract_divide_fusion
  (43 shorter events, 0.6 us)
Async XLA Ops:
  7.2 4.2 %copy-start.8 = (f32[4,24,4096]{2,1,0:T(8,128)S(1)}, f32[4,24,4096]{2,1,0:T(8,128)}, u32[]{:S(2)}) copy-start(f32[4,24,4096]{2,1,0:T(8,128)} %param.10) | copy-start | bytes 4718596
  7.2 2.3 %copy-start.11 = (s32[16]{0:T(128)S(1)}, s32[16]{0:T(128)}, u32[]{:S(2)}) copy-start(s32[16]{0:T(128)} %param.12) | copy-start | bytes 196
  7.2 88.9 %all-gather.7.cloned.1.call-start = ((), (), s32[]{:S(2)}) async-start(), calls=%async_computation.2 | async-start | bytes 13369344 | tf_op jit(solution)/shard_map/all_gather | solution.py:65
  9.4 126.7 %all-gather.9.cloned.1.call-start = ((), (), s32[]{:S(2)}) async-start(), calls=%async_computation.3 | async-start | bytes 6684672 | tf_op jit(solution)/shard_map/all_gather | solution.py:71
  11.5 11.4 %collective-permute-start.2 = (f32[24,4096]{1,0:T(8,128)S(1)}, f32[24,4096]{1,0:T(8,128)S(1)}, u32[]{:S(2)}, u32[]{:S(2)}) collective-permute-start(f32[24,4096]{1,0:T(8,128)S(1)} %get-tuple-element.42), channel_id=1, source_target_pairs={{0,8},{1,9},{2,10},{3,11},{4,12},{5,13},{6,14},{7,15},{8,0},{9,1},... | collective-permute-start | bytes 1179656 | tf_op jit(solution)/shard_map/ppermute | solution.py:56
  15.1 9.7 %collective-permute-start.3 = (f32[24,4096]{1,0:T(8,128)S(1)}, f32[24,4096]{1,0:T(8,128)S(1)}, u32[]{:S(2)}, u32[]{:S(2)}) collective-permute-start(f32[24,4096]{1,0:T(8,128)S(1)} %get-tuple-element.41), channel_id=1, source_target_pairs={{0,1},{1,0},{2,3},{3,2},{4,5},{5,4},{6,7},{7,6},{8,9},{9,8},{10,11... | collective-permute-start | bytes 1179656 | tf_op jit(solution)/shard_map/ppermute | solution.py:59
  34.0 1.9 %copy-start.10 = (s32[4]{0:T(128)S(1)}, s32[4]{0:T(128)}, u32[]{:S(2)}) copy-start(s32[4]{0:T(128)} %param.11) | copy-start | bytes 52
  40.3 47.1 %collective-permute-start = (f32[128,4096]{0,1:T(8,128)}, f32[128,4096]{0,1:T(8,128)}, u32[]{:S(2)}, u32[]{:S(2)}) collective-permute-start(f32[128,4096]{0,1:T(8,128)} %bitcast_add_fusion.3), channel_id=1, source_target_pairs={{0,8},{1,9},{2,10},{3,11},{4,12},{5,13},{6,14},{7,15},{8,0},{9,1},... | collective-permute-start | bytes 6291464 | tf_op jit(solution)/shard_map/ppermute | solution.py:57
  47.8 46.0 %collective-permute-start.1 = (f32[128,4096]{0,1:T(8,128)}, f32[128,4096]{0,1:T(8,128)}, u32[]{:S(2)}, u32[]{:S(2)}) collective-permute-start(f32[128,4096]{0,1:T(8,128)} %bitcast_add_fusion.2), channel_id=1, source_target_pairs={{0,1},{1,0},{2,3},{3,2},{4,5},{5,4},{6,7},{7,6},{8,9},{9,8},{10,11... | collective-permute-start | bytes 6291464 | tf_op jit(solution)/shard_map/ppermute | solution.py:60
  51.0 1.3 copy-start.1
  70.5 3.5 %copy-start = (f32[1,128,4096]{1,2,0:T(8,128)S(1)}, f32[1,128,4096]{1,2,0:T(8,128)}, u32[]{:S(2)}) copy-start(f32[1,128,4096]{1,2,0:T(8,128)} %copy.39) | copy-start | bytes 6291460
  70.5 3.5 %copy-start.3 = (f32[128,64,64]{0,2,1:T(8,128)S(1)}, f32[128,64,64]{0,2,1:T(8,128)}, u32[]{:S(2)}) copy-start(f32[128,64,64]{0,2,1:T(8,128)} %copy.29) | copy-start | bytes 6291460
  74.0 19.9 %copy-start.2 = (f32[1,128,4096]{1,2,0:T(8,128)S(1)}, f32[1,128,4096]{1,2,0:T(8,128)}, u32[]{:S(2)}) copy-start(f32[1,128,4096]{1,2,0:T(8,128)} %copy-done.1) | copy-start | bytes 6291460
  74.0 19.9 %copy-start.7 = (f32[128,64,64]{0,2,1:T(8,128)S(1)}, f32[128,64,64]{0,2,1:T(8,128)}, u32[]{:S(2)}) copy-start(f32[128,64,64]{0,2,1:T(8,128)} %copy.37) | copy-start | bytes 6291460
  75.5 20.6 %copy-start.4 = (f32[1,128,4096]{1,2,0:T(8,128)S(1)}, f32[1,128,4096]{1,2,0:T(8,128)}, u32[]{:S(2)}) copy-start(f32[1,128,4096]{1,2,0:T(8,128)} %bitcast_add_fusion.4) | copy-start | bytes 6291460
  96.1 9.5 %copy-start.5 = (f32[1,128,4096]{1,2,0:T(8,128)S(1)}, f32[1,128,4096]{1,2,0:T(8,128)}, u32[]{:S(2)}) copy-start(f32[1,128,4096]{1,2,0:T(8,128)} %bitcast_add_fusion.5) | copy-start | bytes 6291460
  105.7 30.4 %copy-start.6 = (f32[128,4096]{0,1:T(8,128)S(1)}, f32[128,4096]{0,1:T(8,128)}, u32[]{:S(2)}) copy-start(f32[128,4096]{0,1:T(8,128)} %fusion.11) | copy-start | bytes 6291460
  143.2 6.7 %copy-start.14 = (s32[8,2]{0,1:T(2,128)S(1)}, s32[8,2]{0,1:T(2,128)}, u32[]{:S(2)}) copy-start(s32[8,2]{0,1:T(2,128)} %param.13) | copy-start | bytes 196
  143.2 6.7 %copy-start.13 = (f32[200]{0:T(256)S(1)}, f32[200]{0:T(256)}, u32[]{:S(2)}) copy-start(f32[200]{0:T(256)} %param.14) | copy-start | bytes 2404
  143.2 13.7 %copy-start.12 = (f32[384]{0:T(512)S(1)}, f32[384]{0:T(512)}, u32[]{:S(2)}) copy-start(f32[384]{0:T(512)} %param.15) | copy-start | bytes 4612
  143.2 13.7 %all-to-all-start = ((f32[16,8,384]{2,1,0:T(8,128)}), f32[16,8,384]{2,1,0:T(8,128)S(1)}, u32[]{:S(2)}, u32[]{:S(2)}) async-start(f32[16,8,384]{2,1,0:T(8,128)} %bitcast.42), calls=%async_computation | async-start | bytes 393216 | tf_op jit(solution)/shard_map/all_to_all | solution.py:84
  156.9 0.7 copy-start.9
Sparse Core Ops, SparseCore 0:
  9.8 79.7 all-gather.6
  91.5 44.5 all-gather.8
where the time goes:
time: 165 us; the launch traced here: 164 us
  waiting for transfers between devices  48.7 us (30%)
  local copies, waits for them, and re-layouts  36.9 us (22%)
  matrix products  26.5 us (16%)
  between operations  22 us (13%)
  other arithmetic  15.4 us (9%)
  starting transfers between devices  15 us (9%)
    dot_general x3, matrix products, tile_product(): lax.dot_general(amp_tile, int_rows, (((1,), (1,)), ((), ())), precision=p...  26.5 us
    all_gather x1, waiting for transfers between devices, on_device(): lax.all_gather(third_int, 'pair', axis=0, tiled=True)  20.6 us
    ppermute x1, waiting for transfers between devices, on_device(): recv_amp = lax.ppermute(send_amp, 'virt', perm)  11.9 us
    unnamed x35, local copies, waits for them, and re-layouts  11.2 us
    mul x5, local copies, waits for them, and re-layouts, symmetric_amps(): return amp_rows + flag.astype(jnp.float32) * swap_in_tile(amp_rows)  10 us
    slice x2, local copies, waits for them, and re-layouts, own_amps(): return symmetric_amps(amplitudes[slot], tile_flags[slot])  8.97 us
    add x4, other arithmetic, symmetric_amps(): return amp_rows + flag.astype(jnp.float32) * swap_in_tile(amp_rows)  8.24 us
    all_to_all x1, waiting for transfers between devices, on_device(): received = lax.all_to_all(blocks, 'virt', 0, 0, tiled=False)  6.75 us
  transfers between devices with their start and end apart: 7, of which 6 were waited for; matrix products, arithmetic and copies ran while one was open for 41% of the time, Pallas kernels for 0%

commit v1 on v0

--- a/solution.py
+++ b/solution.py
@@ -68,7 +68,12 @@
     running = running + jnp.where(keep > 1, second, jnp.zeros_like(second))
     third_int = jnp.where(take > 0, recv_int, jnp.where(take_y > 0, recv_int_y, integrals[2]))
     third_amp = jnp.where(take > 0, recv_amp, jnp.where(take_y > 0, recv_amp_y, own_amps(2)))
-    third = tile_product(third_amp, lax.all_gather(third_int, "pair", axis=0, tiled=True))
+    third = tile_product(
+        third_amp,
+        jnp.concatenate(
+            lax.all_to_all(jnp.stack([third_int] * lax.axis_size("pair")), "pair", 0, 0), axis=0
+        ),
+    )
     third_live = (take > 0) | (take_y > 0) | (keep > 2)
     running = running + jnp.where(third_live, third, jnp.zeros_like(third))
 

time: 165 us -> 269 us (1.63)
  waiting for transfers between devices: 48.7 us -> 139 us
  starting transfers between devices: 15 us -> 25.7 us
  local copies, waits for them, and re-layouts: 36.9 us -> 40.3 us
    all_gather x1, waiting for transfers between devices: 0.01 us -> 110 us  [on_device(): first_two = lax.all_gather(integrals[0:2], 'pair', axis=1, tiled=True)]
    all_gather x1 -> x0, waiting for transfers between devices: 20.6 us -> none  [on_device(): lax.all_gather(third_int, 'pair', axis=0, tiled=True)]
    all_to_all x0 -> x1, starting transfers between devices: none -> 10.3 us  [on_device(): lax.all_to_all(jnp.stack([third_int] * lax.axis_size('pair')), 'pair', 0, 0)]
    another operation x0 -> x1, local copies, waits for them, and re-layouts: none -> 3.39 us  [on_device(): jnp.stack([third_int] * lax.axis_size('pair'))]
  transfers between devices with their start and end apart: 7 -> 7, of which waited for: 6 -> 6; matrix products, arithmetic and copies ran while one was open for 41% -> 26% of each run, Pallas kernels for 0% -> 0%
where the time goes in v1:
time: 269 us; the launch traced here: 268 us
  waiting for transfers between devices  139 us (52%)
  local copies, waits for them, and re-layouts  40.3 us (15%)
  matrix products  26.4 us (10%)
  starting transfers between devices  25.7 us (10%)
  between operations  21.9 us (8%)
  other arithmetic  14.2 us (5%)
    all_gather x1, waiting for transfers between devices, on_device(): first_two = lax.all_gather(integrals[0:2], 'pair', axis=1, tiled=True)  110 us
    dot_general x3, matrix products, tile_product(): lax.dot_general(amp_tile, int_rows, (((1,), (1,)), ((), ())), precision=p...  26.4 us
    ppermute x1, waiting for transfers between devices, on_device(): recv_amp = lax.ppermute(send_amp, 'virt', perm)  14.4 us
    unnamed x35, local copies, waits for them, and re-layouts  11.1 us
    all_to_all x1, starting transfers between devices, on_device(): lax.all_to_all(jnp.stack([third_int] * lax.axis_size('pair')), 'pair', 0, 0)  10.3 us
    mul x5, local copies, waits for them, and re-layouts, symmetric_amps(): return amp_rows + flag.astype(jnp.float32) * swap_in_tile(amp_rows)  10.1 us
    slice x2, local copies, waits for them, and re-layouts, own_amps(): return symmetric_amps(amplitudes[slot], tile_flags[slot])  9.12 us
    add x4, other arithmetic, symmetric_amps(): return amp_rows + flag.astype(jnp.float32) * swap_in_tile(amp_rows)  8.01 us
  transfers between devices with their start and end apart: 7, of which 6 were waited for; matrix products, arithmetic and copies ran while one was open for 26% of the time, Pallas kernels for 0%

profile of v1, /device:TPU:1, one launch (start us, length us, event | category | flops | bytes accessed | tf_op | source)
XLA Modules:
  0.0 267.9 jit_solution(8425604484905069004)
XLA Ops:
  7.2 2.2 slice.66
  9.5 0.6 dynamic_slice.27
  11.4 3.6 %collective-permute-start.2 = (f32[24,4096]{1,0:T(8,128)S(1)}, f32[24,4096]{1,0:T(8,128)S(1)}, u32[]{:S(2)}, u32[]{:S(2)}) collective-permute-start(f32[24,4096]{1,0:T(8,128)S(1)} %get-tuple-element.42), channel_id=1, source_target_pairs={{0,8},{1,9},{2,10},{3,11},{4,12},{5,13},{6,14},{7,15},{8,0},{9,1},... | collective-permute-start | bytes 1179656 | tf_op jit(solution)/shard_map/ppermute | solution.py:56
  15.1 1.3 collective-permute-start.3
  16.5 0.6 dynamic_slice.25
  17.1 0.7 gather_fusion
  17.8 0.7 gather_fusion.1
  18.4 0.6 fusion.24
  19.1 0.7 gather_fusion.2
  19.8 0.6 dynamic_slice.26
  21.6 1.3 collective-permute-done.2
  22.9 1.9 collective-permute-done.3
  24.8 3.4 %stack.2 = f32[16,24,4096]{2,1,0:T(8,128)} broadcast(f32[24,4096]{1,0:T(8,128)S(1)} %fusion.21), dimensions={1,2} | broadcast | bytes 6684672 | tf_op jit(solution)/shard_map/stack | solution.py:74
  28.2 10.3 %all-to-all-start = ((f32[16,24,4096]{2,1,0:T(8,128)}), f32[16,24,4096]{2,1,0:T(8,128)}, u32[]{:S(2)}, u32[]{:S(2)}) async-start(f32[16,24,4096]{2,1,0:T(8,128)} %stack.2), calls=%async_computation | async-start | bytes 12582912 | tf_op jit(solution)/shard_map/all_to_all | solution.py:74
  38.5 8.5 %fusion.25 = (f32[1,128,4096]{2,1,0:T(8,128)}, f32[1,128,4096]{2,1,0:T(8,128)}, f32[1,128,4096]{2,1,0:T(8,128)}, f32[1,128,4096]{2,1,0:T(8,128)}, f32[1,128,4096]{2,1,0:T(8,128)}) fusion(f32[4,128,4096]{2,1,0:T(8,128)} %param.9, s32[]{:T(128)S(6)} %select_n.101), kind=kLoop, calls=%fused_computation.59 | loop fusion | bytes 20971524 | tf_op jit(solution)/shard_map/slice | solution.py:63
  47.0 1.9 copy.41
  48.9 0.7 fusion.26
  50.1 0.1 broadcast_multiply_fusion.2
  50.3 1.2 copy.33
  51.5 1.6 bitcast_add_fusion.3
  53.1 1.4 collective-permute-start
  54.5 1.9 copy.42
  57.1 0.1 broadcast_multiply_fusion.1
  57.3 1.2 copy.35
  58.5 1.6 bitcast_add_fusion.2
  60.1 1.3 collective-permute-start.1
  61.5 1.9 copy.43
  64.2 0.5 copy-done.1
  64.7 2.6 copy.37
  67.3 1.9 copy.40
  70.0 2.5 copy.31
  72.5 0.6 dynamic_slice.24
  73.1 2.9 %copy.39 = f32[1,128,4096]{1,2,0:T(8,128)} copy(f32[1,128,4096]{2,1,0:T(8,128)} %get-tuple-element.40) | data formatting | bytes 4194304
  76.6 1.7 broadcast_multiply_fusion.4
  78.4 2.5 copy.29
  82.9 3.3 %bitcast_add_fusion.4 = f32[1,128,4096]{1,2,0:T(8,128)} fusion(f32[1,128,4096]{1,2,0:T(8,128)S(1)} %copy.40, f32[128,64,64]{0,2,1:T(8,128)} %copy.31), kind=kLoop, calls=%fused_computation.19 | loop fusion | flops 524288 | bytes 6291456 | tf_op jit(solution)/shard_map/add | solution.py:15
  86.2 1.5 bitcast_add_fusion.5
  87.7 14.4 %collective-permute-done = f32[128,4096]{0,1:T(8,128)} collective-permute-done((f32[128,4096]{0,1:T(8,128)}, f32[128,4096]{0,1:T(8,128)}, u32[]{:S(2)}, u32[]{:S(2)}) %collective-permute-start) | collective-permute-done | bytes 2097184 | tf_op jit(solution)/shard_map/ppermute | solution.py:57
  102.0 5.1 %collective-permute-done.1 = f32[128,4096]{0,1:T(8,128)} collective-permute-done((f32[128,4096]{0,1:T(8,128)}, f32[128,4096]{0,1:T(8,128)}, u32[]{:S(2)}, u32[]{:S(2)}) %collective-permute-start.1) | collective-permute-done | bytes 2097184 | tf_op jit(solution)/shard_map/ppermute | solution.py:60
  107.2 2.2 fusion.11
  109.4 109.9 %all-gather.6.cloned.1.call-done = f32[2,384,4096]{2,1,0:T(8,128)} async-done(((f32[2,24,4096]{2,1,0:T(8,128)}), f32[2,384,4096]{2,1,0:T(8,128)}) %all-gather.6.cloned.1.call-update) | async-done | bytes 12582928 | tf_op jit(solution)/shard_map/all_gather | solution.py:65
  219.2 9.5 %fusion.17 = f32[128,384]{1,0:T(8,128)S(1)} fusion(f32[2,384,4096]{2,1,0:T(8,128)} %all-gather.6.cloned.1.call-done, f32[1,128,4096]{1,2,0:T(8,128)S(1)} %copy-done.4, pred[]{:T(512)S(6)} %gt.29), kind=kOutput, calls=%fused_computation.23 | convolution fusion | flops 2415968256 | bytes 8585217 | tf_op jit(solution)/shard_map/dot_general | solution.py:19
  228.8 9.7 %fusion.14 = f32[128,384]{1,0:T(8,128)S(1)} fusion(f32[128,384]{1,0:T(8,128)S(1)} %fusion.17, f32[2,384,4096]{2,1,0:T(8,128)} %all-gather.6.cloned.1.call-done, f32[1,128,4096]{1,2,0:T(8,128)S(1)} %copy-done.5), kind=kOutput, calls=%fused_computation.22 | convolution fusion | flops 2415968256 | bytes 8781824 | tf_op jit(solution)/shard_map/dot_general | solution.py:19
  238.5 7.1 %fusion.20 = f32[128,384]{1,0:T(8,128)} fusion(f32[128,384]{1,0:T(8,128)S(1)} %fusion.14, f32[128,4096]{0,1:T(8,128)S(1)} %copy-done.6, f32[384,4096]{1,0:T(8,128)} %bitcast.42, pred[]{:T(512)S(6)} %or.7), kind=kOutput, calls=%fused_computation.25 | convolution fusion | flops 1208057856 | bytes 8781825 | tf_op jit(solution)/shard_map/dot_general | solution.py:19
  245.6 7.7 %all-to-all-start.1 = ((f32[16,8,384]{2,1,0:T(8,128)}), f32[16,8,384]{2,1,0:T(8,128)S(1)}, u32[]{:S(2)}, u32[]{:S(2)}) async-start(f32[16,8,384]{2,1,0:T(8,128)} %bitcast.43), calls=%async_computation.1 | async-start | bytes 393216 | tf_op jit(solution)/shard_map/all_to_all | solution.py:89
  253.4 0.2 select_reduce_fusion.1
  253.6 6.8 %all-to-all-done.1 = f32[16,8,384]{2,1,0:T(8,128)S(1)} async-done(((f32[16,8,384]{2,1,0:T(8,128)}), f32[16,8,384]{2,1,0:T(8,128)S(1)}, u32[]{:S(2)}, u32[]{:S(2)}) %all-to-all-start.1) | async-done | bytes 196640 | tf_op jit(solution)/shard_map/all_to_all | solution.py:89
  260.4 0.7 subtract_divide_fusion
  (43 shorter events, 0.7 us)
Async XLA Ops:
  7.2 4.2 %copy-start.8 = (f32[4,24,4096]{2,1,0:T(8,128)S(1)}, f32[4,24,4096]{2,1,0:T(8,128)}, u32[]{:S(2)}) copy-start(f32[4,24,4096]{2,1,0:T(8,128)} %param.10) | copy-start | bytes 4718596
  7.2 2.3 copy-start.11
  7.2 212.0 %all-gather.6.cloned.1.call-start = ((), (), s32[]{:S(2)}) async-start(), calls=%async_computation.3 | async-start | bytes 13369344 | tf_op jit(solution)/shard_map/all_gather | solution.py:65
  11.4 11.4 %collective-permute-start.2 = (f32[24,4096]{1,0:T(8,128)S(1)}, f32[24,4096]{1,0:T(8,128)S(1)}, u32[]{:S(2)}, u32[]{:S(2)}) collective-permute-start(f32[24,4096]{1,0:T(8,128)S(1)} %get-tuple-element.42), channel_id=1, source_target_pairs={{0,8},{1,9},{2,10},{3,11},{4,12},{5,13},{6,14},{7,15},{8,0},{9,1},... | collective-permute-start | bytes 1179656 | tf_op jit(solution)/shard_map/ppermute | solution.py:56
  15.1 9.7 %collective-permute-start.3 = (f32[24,4096]{1,0:T(8,128)S(1)}, f32[24,4096]{1,0:T(8,128)S(1)}, u32[]{:S(2)}, u32[]{:S(2)}) collective-permute-start(f32[24,4096]{1,0:T(8,128)S(1)} %get-tuple-element.41), channel_id=1, source_target_pairs={{0,1},{1,0},{2,3},{3,2},{4,5},{5,4},{6,7},{7,6},{8,9},{9,8},{10,11... | collective-permute-start | bytes 1179656 | tf_op jit(solution)/shard_map/ppermute | solution.py:59
  28.2 210.3 %all-to-all-start = ((f32[16,24,4096]{2,1,0:T(8,128)}), f32[16,24,4096]{2,1,0:T(8,128)}, u32[]{:S(2)}, u32[]{:S(2)}) async-start(f32[16,24,4096]{2,1,0:T(8,128)} %stack.2), calls=%async_computation | async-start | bytes 12582912 | tf_op jit(solution)/shard_map/all_to_all | solution.py:74
  47.0 1.9 copy-start.10
  53.1 48.9 %collective-permute-start = (f32[128,4096]{0,1:T(8,128)}, f32[128,4096]{0,1:T(8,128)}, u32[]{:S(2)}, u32[]{:S(2)}) collective-permute-start(f32[128,4096]{0,1:T(8,128)} %bitcast_add_fusion.3), channel_id=1, source_target_pairs={{0,8},{1,9},{2,10},{3,11},{4,12},{5,13},{6,14},{7,15},{8,0},{9,1},... | collective-permute-start | bytes 6291464 | tf_op jit(solution)/shard_map/ppermute | solution.py:57
  60.1 47.0 %collective-permute-start.1 = (f32[128,4096]{0,1:T(8,128)}, f32[128,4096]{0,1:T(8,128)}, u32[]{:S(2)}, u32[]{:S(2)}) collective-permute-start(f32[128,4096]{0,1:T(8,128)} %bitcast_add_fusion.2), channel_id=1, source_target_pairs={{0,1},{1,0},{2,3},{3,2},{4,5},{5,4},{6,7},{7,6},{8,9},{9,8},{10,11... | collective-permute-start | bytes 6291464 | tf_op jit(solution)/shard_map/ppermute | solution.py:60
  63.4 1.3 copy-start.1
  82.9 3.3 %copy-start = (f32[1,128,4096]{1,2,0:T(8,128)S(1)}, f32[1,128,4096]{1,2,0:T(8,128)}, u32[]{:S(2)}) copy-start(f32[1,128,4096]{1,2,0:T(8,128)} %copy.39) | copy-start | bytes 6291460
  82.9 3.3 %copy-start.3 = (f32[128,64,64]{0,2,1:T(8,128)S(1)}, f32[128,64,64]{0,2,1:T(8,128)}, u32[]{:S(2)}) copy-start(f32[128,64,64]{0,2,1:T(8,128)} %copy.29) | copy-start | bytes 6291460
  86.2 21.0 %copy-start.2 = (f32[1,128,4096]{1,2,0:T(8,128)S(1)}, f32[1,128,4096]{1,2,0:T(8,128)}, u32[]{:S(2)}) copy-start(f32[1,128,4096]{1,2,0:T(8,128)} %copy-done.1) | copy-start | bytes 6291460
  86.2 21.0 %copy-start.7 = (f32[128,64,64]{0,2,1:T(8,128)S(1)}, f32[128,64,64]{0,2,1:T(8,128)}, u32[]{:S(2)}) copy-start(f32[128,64,64]{0,2,1:T(8,128)} %copy.37) | copy-start | bytes 6291460
  87.7 131.6 %copy-start.4 = (f32[1,128,4096]{1,2,0:T(8,128)S(1)}, f32[1,128,4096]{1,2,0:T(8,128)}, u32[]{:S(2)}) copy-start(f32[1,128,4096]{1,2,0:T(8,128)} %bitcast_add_fusion.4) | copy-start | bytes 6291460
  219.2 9.5 %copy-start.5 = (f32[1,128,4096]{1,2,0:T(8,128)S(1)}, f32[1,128,4096]{1,2,0:T(8,128)}, u32[]{:S(2)}) copy-start(f32[1,128,4096]{1,2,0:T(8,128)} %bitcast_add_fusion.5) | copy-start | bytes 6291460
  228.8 9.8 %copy-start.6 = (f32[128,4096]{0,1:T(8,128)S(1)}, f32[128,4096]{0,1:T(8,128)}, u32[]{:S(2)}) copy-start(f32[128,4096]{0,1:T(8,128)} %fusion.11) | copy-start | bytes 6291460
  245.6 7.7 %copy-start.14 = (s32[8,2]{0,1:T(2,128)S(1)}, s32[8,2]{0,1:T(2,128)}, u32[]{:S(2)}) copy-start(s32[8,2]{0,1:T(2,128)} %param.13) | copy-start | bytes 196
  245.6 7.7 %copy-start.13 = (f32[200]{0:T(256)S(1)}, f32[200]{0:T(256)}, u32[]{:S(2)}) copy-start(f32[200]{0:T(256)} %param.14) | copy-start | bytes 2404
  245.6 14.7 %copy-start.12 = (f32[384]{0:T(512)S(1)}, f32[384]{0:T(512)}, u32[]{:S(2)}) copy-start(f32[384]{0:T(512)} %param.15) | copy-start | bytes 4612
  245.6 14.7 %all-to-all-start.1 = ((f32[16,8,384]{2,1,0:T(8,128)}), f32[16,8,384]{2,1,0:T(8,128)S(1)}, u32[]{:S(2)}, u32[]{:S(2)}) async-start(f32[16,8,384]{2,1,0:T(8,128)} %bitcast.43), calls=%async_computation.1 | async-start | bytes 393216 | tf_op jit(solution)/shard_map/all_to_all | solution.py:89
  260.4 0.7 copy-start.9
Sparse Core Ops, SparseCore 0:
  9.8 209.3 all-gather.5
